TPU v7x, 512 devices: a whole 4x8x8 slice. The times are simulated.
512 devices in a mesh: kv: 16 (over z, core), ep: 32 (over x, y).
Axes of the slice: x: 4, y: 8, z: 8, core: 2. Of those that a mesh axis runs over, the one named last changes fastest.
Arguments:
- queries: bfloat16 [32, 64, 2048], P('ep'), may hold values from -12 to 12
- new_keys: bfloat16 [32, 64, 512], P('ep'), may hold values from -12 to 12
- new_values: bfloat16 [32, 64, 512], P('ep'), may hold values from -6 to 6
- cache_keys: bfloat16 [32, 64, 128, 512], P('ep', 'kv'), may hold values from -12 to 12
- cache_values: bfloat16 [32, 64, 128, 512], P('ep', 'kv'), may hold values from -10 to 10
- page_table: int32 [32, 64], P('ep'), may hold values from 0 to 63, each once within a row
- cached_len: int32 [32], P('ep'), may hold values from 1 to 8192, 65536 in all
- moe_rows: bfloat16 [1024, 4096], P('ep'), may hold values from -6 to 6
- expert_ids: int32 [1024, 2], P('ep'), may hold values from 0 to 7, all different within a row; in each aligned block of 32 rows (0 to 31, 32 to 63, ...) at most 16 rows name the same one
- gate_probs: float32 [1024, 2], P('ep'), may hold values from 0.1 to 0.9
- w_gate: bfloat16 [32, 4096, 2048], P('ep', None, 'kv'), may hold values from -0.09375 to 0.09375
- w_up: bfloat16 [32, 4096, 2048], P('ep', None, 'kv'), may hold values from -0.09375 to 0.09375
- w_down: bfloat16 [32, 2048, 4096], P('ep', 'kv'), may hold values from -0.09375 to 0.09375
Outputs:
- attn_out: bfloat16 [32, 64, 2048], P('ep')
- moe_out: bfloat16 [1024, 4096], P('ep', 'kv')
Inputs may be any that keep to these rules, and one draw needn't show every extreme that they name: `page_table`: each row is a permutation of the 64 slots of its request. `cached_len`: cached positions at or past a request's length hold no data. `expert_ids`: each row names 2 different experts; among the 32 rows of one ep index no expert is named more than 16 times, and this bound is reached.
All inputs are finite; a program needn't handle non-finite values. No bound on the sum of `cached_len` on one device may be relied on, other than what follows from the above.
Results may differ from a plain program's by a relative error of at most 0.0085.
Values may be sent and summed in bfloat16 or wider, within the bound.
No kernel may reach another device: no remote copies, remote signals or barrier semaphores. Data moves between devices by JAX's collectives and lax.ppermute only.
A program may use at most 128 MiB of HBM per device.

v0:
```python
import math
import jax
import jax.numpy as jnp
from jax import lax
from jax.sharding import PartitionSpec as P

HD = 128
EXPERTS = 8
TOP = 2
HQ = 16
KVH = 4
PAGE = 128
POOL_DEV = 4
CAP = 16
ROPE_BASE = 10000.0
MASKED = -1e30


def rotary(values, positions):
    half_width = values.shape[-1] // 2
    indices = jnp.arange(half_width, dtype=jnp.float32)
    frequency = jnp.power(ROPE_BASE, -2.0 * indices / values.shape[-1])
    angles = positions.astype(jnp.float32)[:, None] * frequency[None, :]
    cosine = jnp.cos(angles)[:, None, :]
    sine_part = jnp.sin(angles)[:, None, :]
    lower_half = values[..., :half_width]
    upper_half = values[..., half_width:]
    return jnp.concatenate(
        [
            lower_half * cosine - upper_half * sine_part,
            upper_half * cosine + lower_half * sine_part,
        ],
        axis=-1,
    )


def on_device(
    queries,
    new_keys,
    new_values,
    cache_keys,
    cache_values,
    page_table,
    cached_len,
    moe_rows,
    expert_ids,
    gate_probs,
    w_gate,
    w_up,
    w_down,
):
    kv_index = lax.axis_index("kv")
    kv_count = lax.axis_size("kv")
    all_rows = queries.shape[1]
    block_rows = all_rows // kv_count
    length = cached_len[0]
    group_size = HQ // KVH
    score_scale = 1.0 / math.sqrt(HD)
    slot_ids = kv_index * POOL_DEV + jnp.arange(POOL_DEV, dtype=jnp.int32)
    matches = (page_table[0][:, None] == slot_ids[None, :]).astype(jnp.int32)
    page_index = jnp.sum(
        matches * jnp.arange(page_table.shape[1], dtype=jnp.int32)[:, None], axis=0
    )
    cached_pos = (page_index[:, None] * PAGE + jnp.arange(PAGE, dtype=jnp.int32)[None, :]).reshape(
        -1
    )
    block_start = kv_index * block_rows
    own_pos = length + block_start + jnp.arange(block_rows, dtype=jnp.int32)
    key_block = lax.dynamic_slice_in_dim(new_keys[0], block_start, block_rows, 0)
    value_block = lax.dynamic_slice_in_dim(new_values[0], block_start, block_rows, 0)
    own_keys = rotary(key_block.astype(jnp.float32).reshape(block_rows, KVH, HD), own_pos).astype(
        jnp.bfloat16
    )
    local_keys = jnp.concatenate([cache_keys[0].reshape(-1, KVH, HD), own_keys], axis=0)
    local_values = jnp.concatenate(
        [cache_values[0].reshape(-1, KVH, HD), value_block.reshape(block_rows, KVH, HD)], axis=0
    )
    key_pos = jnp.concatenate([cached_pos, own_pos])
    live_keys = jnp.concatenate([cached_pos < length, jnp.ones((block_rows,), jnp.bool_)])
    positions = length + jnp.arange(all_rows, dtype=jnp.int32)
    rotated = rotary(queries[0].astype(jnp.float32).reshape(all_rows, HQ, HD), positions).astype(
        jnp.bfloat16
    )
    grouped = rotated.reshape(all_rows, KVH, group_size, HD)
    scores = (
        jnp.einsum("nkgd,mkd->nkgm", grouped, local_keys, preferred_element_type=jnp.float32)
        * score_scale
    )
    usable = (live_keys[None, :] & (key_pos[None, :] <= positions[:, None]))[:, None, None, :]
    scores = jnp.where(usable, scores, MASKED)
    part_high = jnp.max(scores, axis=-1)
    highest = lax.pmax(part_high, "kv")
    weights = jnp.where(usable, jnp.exp(scores - highest[..., None]), 0.0)
    part_total = jnp.sum(weights, axis=-1)
    part_blend = jnp.einsum(
        "nkgm,mkd->nkgd",
        weights.astype(jnp.bfloat16),
        local_values,
        preferred_element_type=jnp.float32,
    )
    total_row = jnp.pad(part_total.reshape(1, -1), ((0, 0), (0, HQ * HD - all_rows * HQ)))
    packed = lax.psum(
        jnp.concatenate([part_blend.reshape(all_rows, HQ * HD), total_row], axis=0), "kv"
    )
    row_total = packed[all_rows, : all_rows * HQ].reshape(all_rows, HQ)
    blended = packed[:all_rows].reshape(all_rows, HQ, HD)
    attn_out = (blended / row_total[..., None]).reshape(1, all_rows, HQ * HD).astype(jnp.bfloat16)
    ep_count = lax.axis_size("ep")
    share_count = ep_count // EXPERTS
    tok_rows = moe_rows.shape[0]
    slot_total = ep_count * CAP
    flat_ids = expert_ids.reshape(-1)
    one_hot = (flat_ids[:, None] == jnp.arange(EXPERTS, dtype=jnp.int32)[None, :]).astype(jnp.int32)
    earlier = jnp.cumsum(one_hot, axis=0) - one_hot
    slot_rank = jnp.sum(earlier * one_hot, axis=1)
    slot_index = jnp.arange(slot_total, dtype=jnp.int32)
    dest_expert = slot_index // CAP // share_count
    dest_slot = slot_index % CAP
    matched = (flat_ids[None, :] == dest_expert[:, None]) & (
        slot_rank[None, :] == dest_slot[:, None]
    )
    select = jnp.sum(matched.astype(jnp.float32).reshape(slot_total, tok_rows, TOP), axis=2).astype(
        jnp.bfloat16
    )
    weight_map = jnp.sum(
        jnp.where(matched, gate_probs.reshape(-1)[None, :], 0.0).reshape(slot_total, tok_rows, TOP),
        axis=2,
    )
    col_width = moe_rows.shape[1] // kv_count
    rows_cols = lax.dynamic_slice_in_dim(moe_rows, kv_index * col_width, col_width, 1)
    outgoing = (
        jnp.dot(select, rows_cols, preferred_element_type=jnp.float32)
        .astype(jnp.bfloat16)
        .reshape(ep_count, CAP, -1)
    )
    arrived_cols = lax.all_to_all(outgoing, "ep", split_axis=0, concat_axis=0, tiled=True).reshape(
        slot_total, -1
    )
    arrived = lax.all_gather(arrived_cols, "kv", axis=1, tiled=True)
    gate_proj = jnp.dot(arrived, w_gate[0], preferred_element_type=jnp.float32)
    up_proj = jnp.dot(arrived, w_up[0], preferred_element_type=jnp.float32)
    hidden = (jax.nn.silu(gate_proj) * up_proj).astype(jnp.bfloat16)
    out_width = w_down.shape[2] // kv_count
    down_split = w_down[0].reshape(w_down.shape[1], kv_count, out_width)
    down_cols = lax.all_to_all(down_split, "kv", split_axis=1, concat_axis=0, tiled=True).reshape(
        -1, out_width
    )
    summed = jnp.dot(
        lax.all_gather(hidden, "kv", axis=1, tiled=True),
        down_cols,
        preferred_element_type=jnp.float32,
    )
    returned = (
        lax.all_to_all(
            summed.reshape(ep_count, CAP, -1).astype(jnp.bfloat16),
            "ep",
            split_axis=0,
            concat_axis=0,
            tiled=True,
        )
        .astype(jnp.float32)
        .reshape(slot_total, -1)
    )
    moe_out = jnp.dot(
        weight_map.T, returned, precision=lax.Precision.HIGHEST, preferred_element_type=jnp.float32
    ).astype(jnp.bfloat16)
    return (attn_out, moe_out)


def solution(mesh):
    return jax.shard_map(
        on_device,
        mesh=mesh,
        in_specs=(
            P("ep", None, None),
            P("ep", None, None),
            P("ep", None, None),
            P("ep", "kv", None, None),
            P("ep", "kv", None, None),
            P("ep", None),
            P("ep"),
            P("ep", None),
            P("ep", None),
            P("ep", None),
            P("ep", None, "kv"),
            P("ep", None, "kv"),
            P("ep", "kv", None),
        ),
        out_specs=(P("ep", None, None), P("ep", "kv")),
        check_vma=False,
    )
```

profile of v0, /device:TPU:2, one launch (start us, length us, event | category | flops | bytes accessed | tf_op | source)
XLA Modules:
  0.0 277.6 jit_solution(767339811898479776)
XLA Ops:
  7.2 0.0 copy-start
  7.2 0.0 all-gather.3.cloned.1.call-start
  7.2 0.8 copy.46
  8.1 0.1 eq.71
  8.2 0.1 fusion.26
  8.3 0.1 reduce_window_sum.11
  8.4 0.2 select_reduce_fusion.1
  8.5 0.1 eq.75
  8.7 0.1 copy.47
  8.7 0.8 convert_reduce_fusion
  9.6 1.0 convolution_convert_fusion
  10.5 21.4 %all_to_all.25 = bf16[32,16,256]{2,1,0:T(8,128)(2,1)} all-to-all(bf16[32,16,256]{2,1,0:T(8,128)(2,1)S(1)} %bitcast.94), channel_id=1, replica_groups=mesh['kv'=16,'ep'=32] {'ep'}, dimensions={0} | all-to-all | bytes 524288 | tf_op jit(solution)/shard_map/all_to_all | solution.py:136
  32.0 0.0 all-gather.3.cloned.1.call-update
  32.0 1.5 copy.55
  33.5 0.0 copy-start.4
  33.5 1.3 copy.48
  34.8 10.5 %all-to-all-start.1 = ((bf16[128,16,256]{2,0,1:T(8,128)(2,1)}), bf16[128,16,256]{2,0,1:T(8,128)(2,1)S(1)}, u32[]{:S(2)}, u32[]{:S(2)}) async-start(bf16[128,16,256]{2,0,1:T(8,128)(2,1)} %copy.48), calls=%async_computation.1 | async-start | bytes 2097152 | tf_op jit(solution)/shard_map/all_to_all | solution.py:145
  45.4 0.0 all-gather.5.cloned.1.call-start
  46.1 0.0 copy-done.4
  46.1 0.1 copy.53
  46.2 1.2 reshape_squeeze.10
  47.4 0.9 copy.41
  48.3 0.0 copy-done.6
  48.3 0.2 select_reduce_fusion.2
  48.5 55.1 %all-gather.3.cloned.1.call-done = bf16[512,4096]{1,0:T(8,128)(2,1)} async-done(((bf16[512,256]{1,0:T(8,128)(2,1)}), bf16[512,4096]{1,0:T(8,128)(2,1)}) %all-gather.3.cloned.1.call-update) | async-done | bytes 4194320 | tf_op jit(solution)/shard_map/all_gather | solution.py:139
  103.5 3.6 %fusion.11 = f32[512,128]{1,0:T(8,128)S(1)} fusion(bf16[512,4096]{1,0:T(8,128)(2,1)} %all-gather.3.cloned.1.call-done, bf16[1,4096,128]{2,1,0:T(8,128)(2,1)S(1)} %copy-done), kind=kOutput, calls=%fused_computation.14 | convolution fusion | flops 536870912 | bytes 5505024 | tf_op jit(solution)/shard_map/dot_general | solution.py:140
  107.1 0.1 copy-done.5
  107.3 1.9 fusion.9
  109.2 0.0 all-gather.5.cloned.1.call-update
  109.2 0.0 all-reduce.4.cloned.1.call-start
  109.3 0.1 broadcast_compare_fusion
  109.4 0.1 add_bitcast_fusion
  109.5 0.7 bitcast_convert_fusion
  110.2 0.1 multiply_cosine_fusion.1
  110.3 0.1 compare_and_fusion
  110.4 0.2 multiply_cosine_fusion
  110.6 0.1 subtract_convert_fusion.1
  110.7 0.2 fusion.48
  110.9 0.3 subtract_convert_fusion
  111.2 0.0 copy-start.2
  111.2 2.2 fusion
  113.5 24.3 %pmax.7 = f32[64,4,4]{0,2,1:T(4,128)S(1)} all-reduce(f32[64,4,4]{0,2,1:T(4,128)S(1)} %get-tuple-element.14), channel_id=1, replica_groups=mesh['kv'=16,'ep'=32] {'kv'}, use_global_device_ids=true, to_apply=%region_2.3 | all-reduce | flops 1024 | bytes 8192 | tf_op jit(solution)/shard_map/pmax | solution.py:92
  137.8 2.6 fusion.1
  140.4 0.1 copy.45
  140.5 0.2 reshape.299
  140.7 0.1 reshape_squeeze.9
  140.8 0.1 copy.40
  140.9 0.7 dynamic-slice_bitcast_fusion
  141.6 2.5 fusion.6
  144.1 0.3 copy.44
  144.5 0.2 reshape.298
  144.7 0.9 select_maximum_fusion
  145.6 0.0 all-reduce.4.cloned.1.call-update
  145.6 0.0 all-to-all-done.1
  145.6 3.0 %all-gather.5.cloned.1.call-done = bf16[512,2048]{1,0:T(8,128)(2,1)} async-done(((bf16[512,128]{1,0:T(8,128)(2,1)}), bf16[512,2048]{1,0:T(8,128)(2,1)}) %all-gather.5.cloned.1.call-update) | async-done | bytes 2097168 | tf_op jit(solution)/shard_map/all_gather | solution.py:149
  148.6 3.0 %convolution_convert_fusion.1 = bf16[32,16,256]{2,1,0:T(8,128)(2,1)} fusion(bf16[32,16,2048]{2,1,0:T(8,128)(2,1)} %bitcast.97, bf16[2048,256,1]{1,0,2:T(8,128)(2,1)S(1)} %bitcast.91), kind=kOutput, calls=%fused_computation.9 | convolution fusion | flops 537001984 | bytes 3407872 | tf_op jit(solution)/shard_map/dot_general | solution.py:148
  151.6 9.9 %all-to-all-start.2 = ((bf16[32,16,256]{2,1,0:T(8,128)(2,1)}), bf16[32,16,256]{2,1,0:T(8,128)(2,1)S(1)}, u32[]{:S(2)}, u32[]{:S(2)}) async-start(bf16[32,16,256]{2,1,0:T(8,128)(2,1)} %convolution_convert_fusion.1), calls=%async_computation.2 | async-start | bytes 524288 | tf_op jit(solution)/shard_map/all_to_all | solution.py:154
  161.5 105.7 %all-reduce.4.cloned.1.call-done = f32[65,2048]{1,0:T(8,128)} async-done(((f32[65,2048]{1,0:T(8,128)}), f32[65,2048]{1,0:T(8,128)}) %all-reduce.4.cloned.1.call-update) | async-done | bytes 532496 | tf_op jit(solution)/shard_map/psum | solution.py:102
  267.2 0.8 slice_reduce_fusion
  268.0 0.1 div.45
  268.0 0.2 div.46
  268.2 1.9 fusion.24
  270.2 0.0 all-to-all-done.2
  270.2 0.9 convolution_convert_fusion.2
  (17 shorter events, 0.1 us)
Async XLA Ops:
  7.2 96.4 %copy-start = (bf16[1,4096,128]{2,1,0:T(8,128)(2,1)S(1)}, bf16[1,4096,128]{2,1,0:T(8,128)(2,1)}, u32[]{:S(2)}) copy-start(bf16[1,4096,128]{2,1,0:T(8,128)(2,1)} %param.23) | copy-start | bytes 3145732
  7.2 96.3 %all-gather.3.cloned.1.call-start = ((), (), s32[]{:S(2)}) async-start(), calls=%async_computation.4 | async-start | bytes 4456448 | tf_op jit(solution)/shard_map/all_gather | solution.py:139
  33.5 12.6 %copy-start.4 = (bf16[1,64,2048]{2,1,0:T(8,128)(2,1)S(1)}, bf16[1,64,2048]{2,1,0:T(8,128)(2,1)}, u32[]{:S(2)}) copy-start(bf16[1,64,2048]{2,1,0:T(8,128)(2,1)} %param.13) | copy-start | bytes 786436
  34.8 13.5 %copy-start.6 = (s32[1,64]{1,0:T(1,128)S(1)}, s32[1,64]{1,0:T(1,128)}, u32[]{:S(2)}) copy-start(s32[1,64]{1,0:T(1,128)} %param.18) | copy-start | bytes 772
  34.8 110.8 %all-to-all-start.1 = ((bf16[128,16,256]{2,0,1:T(8,128)(2,1)}), bf16[128,16,256]{2,0,1:T(8,128)(2,1)S(1)}, u32[]{:S(2)}, u32[]{:S(2)}) async-start(bf16[128,16,256]{2,0,1:T(8,128)(2,1)} %copy.48), calls=%async_computation.1 | async-start | bytes 2097152 | tf_op jit(solution)/shard_map/all_to_all | solution.py:145
  45.4 103.2 %all-gather.5.cloned.1.call-start = ((), (), s32[]{:S(2)}) async-start(), calls=%async_computation.5 | async-start | bytes 2228224 | tf_op jit(solution)/shard_map/all_gather | solution.py:149
  103.5 3.6 %copy-start.1 = (bf16[512,4096]{1,0:T(8,128)(2,1)S(1)}, bf16[512,4096]{1,0:T(8,128)(2,1)}, u32[]{:S(2)}) copy-start(bf16[512,4096]{1,0:T(8,128)(2,1)} %all-gather.3.cloned.1.call-done) | copy-start | bytes 12582916
  103.5 3.7 %copy-start.5 = (bf16[1,4096,128]{2,1,0:T(8,128)(2,1)S(1)}, bf16[1,4096,128]{2,1,0:T(8,128)(2,1)}, u32[]{:S(2)}) copy-start(bf16[1,4096,128]{2,1,0:T(8,128)(2,1)} %param.24) | copy-start | bytes 3145732
  109.2 2.0 copy-start.3
  109.2 158.0 %all-reduce.4.cloned.1.call-start = ((), (), s32[]{:S(2)}) async-start(), calls=%async_computation.3 | async-start | bytes 1179648 | tf_op jit(solution)/shard_map/psum | solution.py:102
  111.2 29.5 %copy-start.2 = (bf16[1,4,128,512]{3,2,1,0:T(8,128)(2,1)S(1)}, bf16[1,4,128,512]{3,2,1,0:T(8,128)(2,1)}, u32[]{:S(2)}) copy-start(bf16[1,4,128,512]{3,2,1,0:T(8,128)(2,1)} %param.17) | copy-start | bytes 1572868
  151.6 118.6 %all-to-all-start.2 = ((bf16[32,16,256]{2,1,0:T(8,128)(2,1)}), bf16[32,16,256]{2,1,0:T(8,128)(2,1)S(1)}, u32[]{:S(2)}, u32[]{:S(2)}) async-start(bf16[32,16,256]{2,1,0:T(8,128)(2,1)} %convolution_convert_fusion.1), calls=%async_computation.2 | async-start | bytes 524288 | tf_op jit(solution)/shard_map/all_to_all | solution.py:154
Sparse Core Ops, SparseCore 0:
  32.1 71.3 all-gather.2
  109.3 39.2 all-gather.4
  150.9 116.2 all-reduce.3
where the time goes:
time: 278 us
  waiting for transfers between devices  164 us (59%)
  blocking collectives  45.7 us (16%)
  starting transfers between devices  20.6 us (7%)
  matrix products  15 us (5%)
  between operations  14.7 us (5%)
  local copies, waits for them, and re-layouts  9.25 us (3%)
  other arithmetic  8.53 us (3%)
    psum x1, waiting for transfers between devices, on_device(): lax.psum(jnp.concatenate([part_blend.reshape(all_rows, HQ * HD), total_ro...  106 us
    all_gather x1, waiting for transfers between devices, on_device(): arrived = lax.all_gather(arrived_cols, 'kv', axis=1, tiled=True)  55.1 us
    pmax x1, blocking collectives, on_device(): highest = lax.pmax(part_high, 'kv')  24.3 us
    all_to_all x1, blocking collectives, on_device(): lax.all_to_all(outgoing, 'ep', split_axis=0, concat_axis=0, tiled=True)  21.4 us
    all_to_all x1, starting transfers between devices, on_device(): lax.all_to_all(down_split, 'kv', split_axis=1, concat_axis=0, tiled=True)  10.5 us
    all_to_all x1, starting transfers between devices, on_device(): lax.all_to_all(summed.reshape(ep_count, CAP, -1).astype(jnp.bfloat16), 'e...  9.89 us
  transfers between devices with their start and end apart: 5, of which 3 were waited for; matrix products, arithmetic and copies ran while one was open for 10% of the time, Pallas kernels for 0%

commit v1 on v0

--- a/solution.py
+++ b/solution.py
@@ -136,7 +136,21 @@
     arrived_cols = lax.all_to_all(outgoing, "ep", split_axis=0, concat_axis=0, tiled=True).reshape(
         slot_total, -1
     )
-    arrived = lax.all_gather(arrived_cols, "kv", axis=1, tiled=True)
+    ways, here, step = (lax.axis_size("kv"), lax.axis_index("kv"), arrived_cols.shape[1])
+    shape = [n * ways if d == 1 else n for d, n in enumerate(arrived_cols.shape)]
+    full = lax.dynamic_update_slice_in_dim(
+        jnp.zeros(shape, arrived_cols.dtype), arrived_cols, here * step, axis=1
+    )
+    going_up = going_down = arrived_cols
+    for far in range(1, ways // 2 + 1):
+        going_up = lax.ppermute(going_up, "kv", [(d, (d + 1) % ways) for d in range(ways)])
+        full = lax.dynamic_update_slice_in_dim(full, going_up, (here - far) % ways * step, axis=1)
+        if 2 * far < ways:
+            going_down = lax.ppermute(going_down, "kv", [(d, (d - 1) % ways) for d in range(ways)])
+            full = lax.dynamic_update_slice_in_dim(
+                full, going_down, (here + far) % ways * step, axis=1
+            )
+    arrived = full
     gate_proj = jnp.dot(arrived, w_gate[0], preferred_element_type=jnp.float32)
     up_proj = jnp.dot(arrived, w_up[0], preferred_element_type=jnp.float32)
     hidden = (jax.nn.silu(gate_proj) * up_proj).astype(jnp.bfloat16)

time: 278 us -> 296 us (1.065)
  starting transfers between devices: 20.6 us -> 41.4 us
  waiting for transfers between devices: 164 us -> 154 us
  local copies, waits for them, and re-layouts: 9.25 us -> 16.1 us
    all_gather x1 -> x0, waiting for transfers between devices: 55.1 us -> none  [on_device(): arrived = lax.all_gather(arrived_cols, 'kv', axis=1, tiled=True)]
    ppermute x0 -> x15, waiting for transfers between devices: none -> 45.5 us  [the longest x7 27.6 us: on_device(): lax.ppermute(going_down, 'kv', [(d, (d - 1) % ways) for d in range(ways)])]
    ppermute x0 -> x15, starting transfers between devices: none -> 23.3 us  [the longest x7 23.3 us: on_device(): lax.ppermute(going_down, 'kv', [(d, (d - 1) % ways) for d in range(ways)])]
    dynamic_update_slice x0 -> x16, local copies, waits for them, and re-layouts: none -> 4.2 us  [the longest x8 2.1 us: on_device(): lax.dynamic_update_slice_in_dim(full, going_up, (here - far) % ways * ste...]
  transfers between devices with their start and end apart: 5 -> 19, of which waited for: 3 -> 12; matrix products, arithmetic and copies ran while one was open for 10% -> 12% of each run, Pallas kernels for 0% -> 0%
where the time goes in v1:
time: 296 us; the launch traced here: 295 us
  waiting for transfers between devices  154 us (52%)
  blocking collectives  45.7 us (15%)
  starting transfers between devices  41.4 us (14%)
  local copies, waits for them, and re-layouts  16.1 us (5%)
  between operations  15.4 us (5%)
  matrix products  13.9 us (5%)
  other arithmetic  8.53 us (3%)
    psum x1, waiting for transfers between devices, on_device(): lax.psum(jnp.concatenate([part_blend.reshape(all_rows, HQ * HD), total_ro...  105 us
    ppermute x7, waiting for transfers between devices, on_device(): lax.ppermute(going_down, 'kv', [(d, (d - 1) % ways) for d in range(ways)])  27.6 us
    pmax x1, blocking collectives, on_device(): highest = lax.pmax(part_high, 'kv')  24.4 us
    ppermute x7, starting transfers between devices, on_device(): lax.ppermute(going_down, 'kv', [(d, (d - 1) % ways) for d in range(ways)])  23.3 us
    all_to_all x1, blocking collectives, on_device(): lax.all_to_all(outgoing, 'ep', split_axis=0, concat_axis=0, tiled=True)  21.3 us
    ppermute x8, waiting for transfers between devices, on_device(): lax.ppermute(going_up, 'kv', [(d, (d + 1) % ways) for d in range(ways)])  18 us
    all_to_all x1, starting transfers between devices, on_device(): lax.all_to_all(summed.reshape(ep_count, CAP, -1).astype(jnp.bfloat16), 'e...  9.86 us
    all_to_all x1, starting transfers between devices, on_device(): lax.all_to_all(down_split, 'kv', split_axis=1, concat_axis=0, tiled=True)  8.11 us
  transfers between devices with their start and end apart: 19, of which 12 were waited for; matrix products, arithmetic and copies ran while one was open for 12% of the time, Pallas kernels for 0%

profile of v1, /device:TPU:2, one launch (start us, length us, event | category | flops | bytes accessed | tf_op | source)
XLA Modules:
  0.0 295.4 jit_solution(5883411364777420252)
XLA Ops:
  7.2 0.9 copy.46
  8.1 0.1 eq.87
  8.3 0.1 reduce_window_sum.11
  8.4 0.2 select_reduce_fusion.1
  8.5 0.1 eq.91
  8.7 0.8 convert_reduce_fusion
  9.6 1.0 convolution_convert_fusion
  10.5 21.3 %all_to_all.25 = bf16[32,16,256]{2,1,0:T(8,128)(2,1)S(1)} all-to-all(bf16[32,16,256]{2,1,0:T(8,128)(2,1)S(1)} %bitcast.100), channel_id=1, replica_groups=mesh['kv'=16,'ep'=32] {'ep'}, dimensions={0} | all-to-all | bytes 524288 | tf_op jit(solution)/shard_map/all_to_all | solution.py:136
  31.8 5.4 %collective-permute-start.1 = (bf16[512,256]{1,0:T(8,128)(2,1)S(1)}, bf16[512,256]{1,0:T(8,128)(2,1)S(1)}, u32[]{:S(2)}, u32[]{:S(2)}) collective-permute-start(bf16[512,256]{1,0:T(8,128)(2,1)S(1)} %bitcast.95), channel_id=1, source_target_pairs={{0,480},{32,0},{64,32},{96,64},{128,96},{160,128},{192,160},{224,1... | collective-permute-start | bytes 786440 | tf_op jit(solution)/shard_map/ppermute | solution.py:149
  37.3 4.1 %collective-permute-done = bf16[512,256]{1,0:T(8,128)(2,1)S(1)} collective-permute-done((bf16[512,256]{1,0:T(8,128)(2,1)S(1)}, bf16[512,256]{1,0:T(8,128)(2,1)S(1)}, u32[]{:S(2)}, u32[]{:S(2)}) %collective-permute-start) | collective-permute-done | bytes 262176 | tf_op jit(solution)/shard_map/ppermute | solution.py:146
  41.3 1.6 copy.55
  42.9 1.3 copy.48
  44.2 8.1 %all-to-all-start.1 = ((bf16[128,16,256]{2,0,1:T(8,128)(2,1)}), bf16[128,16,256]{2,0,1:T(8,128)(2,1)S(1)}, u32[]{:S(2)}, u32[]{:S(2)}) async-start(bf16[128,16,256]{2,0,1:T(8,128)(2,1)} %copy.48), calls=%async_computation.1 | async-start | bytes 2097152 | tf_op jit(solution)/shard_map/all_to_all | solution.py:159
  52.4 2.9 collective-permute-start.3
  55.4 23.3 %collective-permute-done.3 = bf16[512,256]{1,0:T(8,128)(2,1)} collective-permute-done((bf16[512,256]{1,0:T(8,128)(2,1)S(1)}, bf16[512,256]{1,0:T(8,128)(2,1)}, u32[]{:S(2)}, u32[]{:S(2)}) %collective-permute-start.3) | collective-permute-done | bytes 262176 | tf_op jit(solution)/shard_map/ppermute | solution.py:149
  78.6 3.2 %collective-permute-start.5 = (bf16[512,256]{1,0:T(8,128)(2,1)}, bf16[512,256]{1,0:T(8,128)(2,1)}, u32[]{:S(2)}, u32[]{:S(2)}) collective-permute-start(bf16[512,256]{1,0:T(8,128)(2,1)} %collective-permute-done.3), channel_id=1, source_target_pairs={{0,480},{32,0},{64,32},{96,64},{128,96},{160,128},{192,160},{224,1... | collective-permute-start | bytes 786440 | tf_op jit(solution)/shard_map/ppermute | solution.py:149
  81.9 0.2 select_reduce_fusion.2
  83.1 1.2 reshape_squeeze.10
  84.2 0.9 copy.41
  85.1 1.2 reshape_squeeze.9
  86.3 0.9 copy.40
  87.2 0.5 broadcast_in_dim.33
  87.7 0.4 copy-done.5
  88.1 2.6 collective-permute-start.7
  90.8 3.6 %collective-permute-done.6 = bf16[512,256]{1,0:T(8,128)(2,1)S(1)} collective-permute-done((bf16[512,256]{1,0:T(8,128)(2,1)}, bf16[512,256]{1,0:T(8,128)(2,1)S(1)}, u32[]{:S(2)}, u32[]{:S(2)}) %collective-permute-start.6) | collective-permute-done | bytes 262176 | tf_op jit(solution)/shard_map/ppermute | solution.py:146
  94.4 1.0 constant_dynamic-update-slice_fusion.12
  95.4 1.0 constant_dynamic-update-slice_fusion.11
  96.4 3.0 %collective-permute-start.9 = (bf16[512,256]{1,0:T(8,128)(2,1)S(1)}, bf16[512,256]{1,0:T(8,128)(2,1)S(1)}, u32[]{:S(2)}, u32[]{:S(2)}) collective-permute-start(bf16[512,256]{1,0:T(8,128)(2,1)S(1)} %collective-permute-done.7), channel_id=1, source_target_pairs={{0,480},{32,0},{64,32},{96,64},{128,96},{160,128},{192,160},{224,1... | collective-permute-start | bytes 786440 | tf_op jit(solution)/shard_map/ppermute | solution.py:149
  99.3 1.0 constant_dynamic-update-slice_fusion.10
  100.3 1.1 collective-permute-done.8
  101.4 1.0 constant_dynamic-update-slice_fusion.9
  102.4 0.8 collective-permute-done.9
  103.2 3.1 %collective-permute-start.11 = (bf16[512,256]{1,0:T(8,128)(2,1)S(1)}, bf16[512,256]{1,0:T(8,128)(2,1)S(1)}, u32[]{:S(2)}, u32[]{:S(2)}) collective-permute-start(bf16[512,256]{1,0:T(8,128)(2,1)S(1)} %collective-permute-done.9), channel_id=1, source_target_pairs={{0,480},{32,0},{64,32},{96,64},{128,96},{160,128},{192,160},{224,1... | collective-permute-start | bytes 786440 | tf_op jit(solution)/shard_map/ppermute | solution.py:149
  106.4 2.0 collective-permute-done.10
  108.5 1.7 collective-permute-done.11
  110.2 3.1 %collective-permute-start.13 = (bf16[512,256]{1,0:T(8,128)(2,1)S(1)}, bf16[512,256]{1,0:T(8,128)(2,1)S(1)}, u32[]{:S(2)}, u32[]{:S(2)}) collective-permute-start(bf16[512,256]{1,0:T(8,128)(2,1)S(1)} %collective-permute-done.11), channel_id=1, source_target_pairs={{0,480},{32,0},{64,32},{96,64},{128,96},{160,128},{192,160},{224,1... | collective-permute-start | bytes 786440 | tf_op jit(solution)/shard_map/ppermute | solution.py:149
  113.4 2.0 collective-permute-done.12
  115.5 1.8 collective-permute-done.13
  117.3 5.2 %collective-permute-done.14 = bf16[512,256]{1,0:T(8,128)(2,1)S(1)} collective-permute-done((bf16[512,256]{1,0:T(8,128)(2,1)S(1)}, bf16[512,256]{1,0:T(8,128)(2,1)S(1)}, u32[]{:S(2)}, u32[]{:S(2)}) %collective-permute-start.14) | collective-permute-done | bytes 262176 | tf_op jit(solution)/shard_map/ppermute | solution.py:146
  122.5 1.2 fusion.11
  123.7 1.9 multiply_convert_fusion
  125.9 0.7 fusion.31
  126.6 0.1 multiply_cosine_fusion.1
  126.8 0.2 multiply_cosine_fusion
  127.1 0.2 fusion.51
  127.3 0.3 subtract_convert_fusion
  127.7 3.2 %fusion = (f32[64,4,4]{0,2,1:T(4,128)S(1)}, f32[4,516,64,4]{1,2,3,0:T(8,128)}) fusion(pred[64,516]{1,0:T(8,128)(4,1)S(1)} %compare_and_fusion, bf16[64,4,4,64]{3,0,2,1:T(8,128)(2,1)S(1)} %bitcast.102, bf16[64,4,4,64]{3,0,2,1:T(8,128)(2,1)S(1)} %bitcast.101, bf16[4,4,64]{2,0,1:T(4,128)(2,1)S(1)} %get-tuple-element.9, ...), kind=kOutput, calls=%fused_computation.2 | convolution fusion | flops 138959872 | bytes 2941184 | tf_op jit(solution)/shard_map/nkgd,mkd->nkgm/dot_general | solution.py:86
  130.9 24.4 %pmax.7 = f32[64,4,4]{0,2,1:T(4,128)S(1)} all-reduce(f32[64,4,4]{0,2,1:T(4,128)S(1)} %get-tuple-element.14), channel_id=1, replica_groups=mesh['kv'=16,'ep'=32] {'kv'}, use_global_device_ids=true, to_apply=%region_2.3 | all-reduce | flops 1024 | bytes 8192 | tf_op jit(solution)/shard_map/pmax | solution.py:92
  155.3 0.7 fusion.29
  156.0 2.7 fusion.6
  158.7 0.3 copy.44
  159.0 0.2 reshape.298
  159.2 2.6 fusion.1
  161.9 0.1 copy.45
  162.0 0.2 reshape.299
  162.2 0.9 select_maximum_fusion
  163.1 3.3 %all-gather.2.cloned.1.call-done = bf16[512,2048]{1,0:T(8,128)(2,1)} async-done(((bf16[512,128]{1,0:T(8,128)(2,1)}), bf16[512,2048]{1,0:T(8,128)(2,1)}) %all-gather.2.cloned.1.call-update) | async-done | bytes 2097168 | tf_op jit(solution)/shard_map/all_gather | solution.py:163
  166.3 3.0 %convolution_convert_fusion.1 = bf16[32,16,256]{2,1,0:T(8,128)(2,1)} fusion(bf16[32,16,2048]{2,1,0:T(8,128)(2,1)} %bitcast.103, bf16[2048,256,1]{1,0,2:T(8,128)(2,1)S(1)} %bitcast.98), kind=kOutput, calls=%fused_computation.9 | convolution fusion | flops 537001984 | bytes 3407872 | tf_op jit(solution)/shard_map/dot_general | solution.py:162
  169.3 9.9 %all-to-all-start.2 = ((bf16[32,16,256]{2,1,0:T(8,128)(2,1)}), bf16[32,16,256]{2,1,0:T(8,128)(2,1)S(1)}, u32[]{:S(2)}, u32[]{:S(2)}) async-start(bf16[32,16,256]{2,1,0:T(8,128)(2,1)} %convolution_convert_fusion.1), calls=%async_computation.2 | async-start | bytes 524288 | tf_op jit(solution)/shard_map/all_to_all | solution.py:168
  179.2 105.5 %all-reduce.4.cloned.1.call-done = f32[65,2048]{1,0:T(8,128)} async-done(((f32[65,2048]{1,0:T(8,128)}), f32[65,2048]{1,0:T(8,128)}) %all-reduce.4.cloned.1.call-update) | async-done | bytes 532496 | tf_op jit(solution)/shard_map/psum | solution.py:102
  284.7 0.8 slice_reduce_fusion
  285.5 0.2 div.46
  285.7 1.9 fusion.24
  287.7 0.9 convolution_convert_fusion.2
  (63 shorter events, 1.2 us)
Async XLA Ops:
  7.2 115.3 %copy-start = (bf16[1,4096,128]{2,1,0:T(8,128)(2,1)S(1)}, bf16[1,4096,128]{2,1,0:T(8,128)(2,1)}, u32[]{:S(2)}) copy-start(bf16[1,4096,128]{2,1,0:T(8,128)(2,1)} %param.23) | copy-start | bytes 3145732
  7.2 48.1 %copy-start.1 = (bf16[1,64,2048]{2,1,0:T(8,128)(2,1)S(1)}, bf16[1,64,2048]{2,1,0:T(8,128)(2,1)}, u32[]{:S(2)}) copy-start(bf16[1,64,2048]{2,1,0:T(8,128)(2,1)} %param.13) | copy-start | bytes 786436
  7.2 74.7 %copy-start.7 = (s32[1,64]{1,0:T(1,128)S(1)}, s32[1,64]{1,0:T(1,128)}, u32[]{:S(2)}) copy-start(s32[1,64]{1,0:T(1,128)} %param.18) | copy-start | bytes 772
  31.8 9.5 %collective-permute-start = (bf16[512,256]{1,0:T(8,128)(2,1)S(1)}, bf16[512,256]{1,0:T(8,128)(2,1)S(1)}, u32[]{:S(2)}, u32[]{:S(2)}) collective-permute-start(bf16[512,256]{1,0:T(8,128)(2,1)S(1)} %bitcast.94), channel_id=1, source_target_pairs={{0,32},{32,64},{64,96},{96,128},{128,160},{160,192},{192,224},{224... | collective-permute-start | bytes 786440 | tf_op jit(solution)/shard_map/ppermute | solution.py:146
  31.8 20.6 %collective-permute-start.1 = (bf16[512,256]{1,0:T(8,128)(2,1)S(1)}, bf16[512,256]{1,0:T(8,128)(2,1)S(1)}, u32[]{:S(2)}, u32[]{:S(2)}) collective-permute-start(bf16[512,256]{1,0:T(8,128)(2,1)S(1)} %bitcast.95), channel_id=1, source_target_pairs={{0,480},{32,0},{64,32},{96,64},{128,96},{160,128},{192,160},{224,1... | collective-permute-start | bytes 786440 | tf_op jit(solution)/shard_map/ppermute | solution.py:149
  41.3 14.0 %copy-start.4 = (bf16[512,256]{1,0:T(8,128)(2,1)}, bf16[512,256]{1,0:T(8,128)(2,1)S(1)}, u32[]{:S(2)}) copy-start(bf16[512,256]{1,0:T(8,128)(2,1)S(1)} %collective-permute-done) | copy-start | bytes 786436
  41.3 14.0 %collective-permute-start.2 = (bf16[512,256]{1,0:T(8,128)(2,1)S(1)}, bf16[512,256]{1,0:T(8,128)(2,1)}, u32[]{:S(2)}, u32[]{:S(2)}) collective-permute-start(bf16[512,256]{1,0:T(8,128)(2,1)S(1)} %collective-permute-done), channel_id=1, source_target_pairs={{0,32},{32,64},{64,96},{96,128},{128,160},{160,192},{192,224},{224... | collective-permute-start | bytes 786440 | tf_op jit(solution)/shard_map/ppermute | solution.py:146
  44.2 118.8 %all-to-all-start.1 = ((bf16[128,16,256]{2,0,1:T(8,128)(2,1)}), bf16[128,16,256]{2,0,1:T(8,128)(2,1)S(1)}, u32[]{:S(2)}, u32[]{:S(2)}) async-start(bf16[128,16,256]{2,0,1:T(8,128)(2,1)} %copy.48), calls=%async_computation.1 | async-start | bytes 2097152 | tf_op jit(solution)/shard_map/all_to_all | solution.py:159
  52.4 114.0 %all-gather.2.cloned.1.call-start = ((), (), s32[]{:S(2)}) async-start(), calls=%async_computation.4 | async-start | bytes 2228224 | tf_op jit(solution)/shard_map/all_gather | solution.py:163
  52.4 30.5 %copy-start.2 = (bf16[512,256]{1,0:T(8,128)(2,1)}, bf16[512,256]{1,0:T(8,128)(2,1)S(1)}, u32[]{:S(2)}) copy-start(bf16[512,256]{1,0:T(8,128)(2,1)S(1)} %collective-permute-done.1) | copy-start | bytes 786436
  52.4 26.2 %collective-permute-start.3 = (bf16[512,256]{1,0:T(8,128)(2,1)S(1)}, bf16[512,256]{1,0:T(8,128)(2,1)}, u32[]{:S(2)}, u32[]{:S(2)}) collective-permute-start(bf16[512,256]{1,0:T(8,128)(2,1)S(1)} %collective-permute-done.1), channel_id=1, source_target_pairs={{0,480},{32,0},{64,32},{96,64},{128,96},{160,128},{192,160},{224,1... | collective-permute-start | bytes 786440 | tf_op jit(solution)/shard_map/ppermute | solution.py:149
  55.3 31.8 %collective-permute-start.4 = (bf16[512,256]{1,0:T(8,128)(2,1)}, bf16[512,256]{1,0:T(8,128)(2,1)}, u32[]{:S(2)}, u32[]{:S(2)}) collective-permute-start(bf16[512,256]{1,0:T(8,128)(2,1)} %collective-permute-done.2), channel_id=1, source_target_pairs={{0,32},{32,64},{64,96},{96,128},{128,160},{160,192},{192,224},{224... | collective-permute-start | bytes 786440 | tf_op jit(solution)/shard_map/ppermute | solution.py:146
  78.6 9.5 %collective-permute-start.5 = (bf16[512,256]{1,0:T(8,128)(2,1)}, bf16[512,256]{1,0:T(8,128)(2,1)}, u32[]{:S(2)}, u32[]{:S(2)}) collective-permute-start(bf16[512,256]{1,0:T(8,128)(2,1)} %collective-permute-done.3), channel_id=1, source_target_pairs={{0,480},{32,0},{64,32},{96,64},{128,96},{160,128},{192,160},{224,1... | collective-permute-start | bytes 786440 | tf_op jit(solution)/shard_map/ppermute | solution.py:149
  87.1 0.9 copy-start.5
  87.2 3.6 %copy-start.3 = (bf16[512,256]{1,0:T(8,128)(2,1)S(1)}, bf16[512,256]{1,0:T(8,128)(2,1)}, u32[]{:S(2)}) copy-start(bf16[512,256]{1,0:T(8,128)(2,1)} %copy-done.2) | copy-start | bytes 786436
  87.2 7.2 %collective-permute-start.6 = (bf16[512,256]{1,0:T(8,128)(2,1)}, bf16[512,256]{1,0:T(8,128)(2,1)S(1)}, u32[]{:S(2)}, u32[]{:S(2)}) collective-permute-start(bf16[512,256]{1,0:T(8,128)(2,1)} %collective-permute-done.4), channel_id=1, source_target_pairs={{0,32},{32,64},{64,96},{96,128},{128,160},{160,192},{192,224},{224... | collective-permute-start | bytes 786440 | tf_op jit(solution)/shard_map/ppermute | solution.py:146
  88.1 8.2 %collective-permute-start.7 = (bf16[512,256]{1,0:T(8,128)(2,1)}, bf16[512,256]{1,0:T(8,128)(2,1)S(1)}, u32[]{:S(2)}, u32[]{:S(2)}) collective-permute-start(bf16[512,256]{1,0:T(8,128)(2,1)} %collective-permute-done.5), channel_id=1, source_target_pairs={{0,480},{32,0},{64,32},{96,64},{128,96},{160,128},{192,160},{224,1... | collective-permute-start | bytes 786440 | tf_op jit(solution)/shard_map/ppermute | solution.py:149
  94.4 7.0 %collective-permute-start.8 = (bf16[512,256]{1,0:T(8,128)(2,1)S(1)}, bf16[512,256]{1,0:T(8,128)(2,1)S(1)}, u32[]{:S(2)}, u32[]{:S(2)}) collective-permute-start(bf16[512,256]{1,0:T(8,128)(2,1)S(1)} %collective-permute-done.6), channel_id=1, source_target_pairs={{0,32},{32,64},{64,96},{96,128},{128,160},{160,192},{192,224},{224... | collective-permute-start | bytes 786440 | tf_op jit(solution)/shard_map/ppermute | solution.py:146
  96.4 6.9 %collective-permute-start.9 = (bf16[512,256]{1,0:T(8,128)(2,1)S(1)}, bf16[512,256]{1,0:T(8,128)(2,1)S(1)}, u32[]{:S(2)}, u32[]{:S(2)}) collective-permute-start(bf16[512,256]{1,0:T(8,128)(2,1)S(1)} %collective-permute-done.7), channel_id=1, source_target_pairs={{0,480},{32,0},{64,32},{96,64},{128,96},{160,128},{192,160},{224,1... | collective-permute-start | bytes 786440 | tf_op jit(solution)/shard_map/ppermute | solution.py:149
  101.4 7.0 %collective-permute-start.10 = (bf16[512,256]{1,0:T(8,128)(2,1)S(1)}, bf16[512,256]{1,0:T(8,128)(2,1)S(1)}, u32[]{:S(2)}, u32[]{:S(2)}) collective-permute-start(bf16[512,256]{1,0:T(8,128)(2,1)S(1)} %collective-permute-done.8), channel_id=1, source_target_pairs={{0,32},{32,64},{64,96},{96,128},{128,160},{160,192},{192,224},{224... | collective-permute-start | bytes 786440 | tf_op jit(solution)/shard_map/ppermute | solution.py:146
  103.2 7.0 %collective-permute-start.11 = (bf16[512,256]{1,0:T(8,128)(2,1)S(1)}, bf16[512,256]{1,0:T(8,128)(2,1)S(1)}, u32[]{:S(2)}, u32[]{:S(2)}) collective-permute-start(bf16[512,256]{1,0:T(8,128)(2,1)S(1)} %collective-permute-done.9), channel_id=1, source_target_pairs={{0,480},{32,0},{64,32},{96,64},{128,96},{160,128},{192,160},{224,1... | collective-permute-start | bytes 786440 | tf_op jit(solution)/shard_map/ppermute | solution.py:149
  108.4 7.0 %collective-permute-start.12 = (bf16[512,256]{1,0:T(8,128)(2,1)S(1)}, bf16[512,256]{1,0:T(8,128)(2,1)S(1)}, u32[]{:S(2)}, u32[]{:S(2)}) collective-permute-start(bf16[512,256]{1,0:T(8,128)(2,1)S(1)} %collective-permute-done.10), channel_id=1, source_target_pairs={{0,32},{32,64},{64,96},{96,128},{128,160},{160,192},{192,224},{224... | collective-permute-start | bytes 786440 | tf_op jit(solution)/shard_map/ppermute | solution.py:146
  108.5 15.2 %copy-start.6 = (bf16[1,4096,128]{2,1,0:T(8,128)(2,1)S(1)}, bf16[1,4096,128]{2,1,0:T(8,128)(2,1)}, u32[]{:S(2)}) copy-start(bf16[1,4096,128]{2,1,0:T(8,128)(2,1)} %param.24) | copy-start | bytes 3145732
  110.2 7.0 %collective-permute-start.13 = (bf16[512,256]{1,0:T(8,128)(2,1)S(1)}, bf16[512,256]{1,0:T(8,128)(2,1)S(1)}, u32[]{:S(2)}, u32[]{:S(2)}) collective-permute-start(bf16[512,256]{1,0:T(8,128)(2,1)S(1)} %collective-permute-done.11), channel_id=1, source_target_pairs={{0,480},{32,0},{64,32},{96,64},{128,96},{160,128},{192,160},{224,1... | collective-permute-start | bytes 786440 | tf_op jit(solution)/shard_map/ppermute | solution.py:149
  115.4 7.0 %collective-permute-start.14 = (bf16[512,256]{1,0:T(8,128)(2,1)S(1)}, bf16[512,256]{1,0:T(8,128)(2,1)S(1)}, u32[]{:S(2)}, u32[]{:S(2)}) collective-permute-start(bf16[512,256]{1,0:T(8,128)(2,1)S(1)} %collective-permute-done.12), channel_id=1, source_target_pairs={{0,32},{32,64},{64,96},{96,128},{128,160},{160,192},{192,224},{224... | collective-permute-start | bytes 786440 | tf_op jit(solution)/shard_map/ppermute | solution.py:146
  125.7 159.0 %all-reduce.4.cloned.1.call-start = ((), (), s32[]{:S(2)}) async-start(), calls=%async_computation.3 | async-start | bytes 1179648 | tf_op jit(solution)/shard_map/psum | solution.py:102
  169.3 118.4 %all-to-all-start.2 = ((bf16[32,16,256]{2,1,0:T(8,128)(2,1)}), bf16[32,16,256]{2,1,0:T(8,128)(2,1)S(1)}, u32[]{:S(2)}, u32[]{:S(2)}) async-start(bf16[32,16,256]{2,1,0:T(8,128)(2,1)} %convolution_convert_fusion.1), calls=%async_computation.2 | async-start | bytes 524288 | tf_op jit(solution)/shard_map/all_to_all | solution.py:168
Sparse Core Ops, SparseCore 0:
  125.8 40.4 all-gather.1
  168.7 115.9 all-reduce.3
